TPU v7x, 256 devices: a whole 4x4x8 slice. The times are simulated.
256 devices in a mesh: req: 64 (over y, z_lo, x, core), tp: 4 (over z_hi).
Axes of the slice: x: 4, y: 4, z: 8 (z_hi: 4, z_lo: 2; z = z_hi * 2 + z_lo), core: 2. Of those that a mesh axis runs over, the one named last changes fastest.
Arguments:
- tokens: bfloat16 [16384, 2048], P('req'), may hold values from -6 to 6
- norm_gain: float32 [2048], replicated, may hold values from 0.25 to 1.75
- w_query: bfloat16 [2048, 2048], P(None, 'tp'), may hold values from -1 to 1
- w_key: bfloat16 [2048, 2048], P(None, 'tp'), may hold values from -1 to 1
- w_value: bfloat16 [2048, 2048], P(None, 'tp'), may hold values from -0.125 to 0.125
- w_out: bfloat16 [2048, 2048], P('tp'), may hold values from -0.125 to 0.125
- lambdas: float32 [4, 8, 128], P(None, 'tp'), may hold values from -1 to 1
- sub_gain: float32 [8, 256], P('tp'), may hold values from 0.5 to 2
- lengths: int32 [4], replicated, may hold values from 1 to 8192, 16384 in all
Outputs:
- hidden: bfloat16 [16384, 2048], P('req')
- key_cache: bfloat16 [16384, 2048], P('req', 'tp')
- value_cache: bfloat16 [16384, 2048], P('req', 'tp')
Inputs may be any that keep to these rules, and one draw needn't show every extreme that they name: The lengths sum to 16384; the longest is exactly 8192.
All inputs are finite; a program needn't handle non-finite values.
Results may differ from a plain program's by a relative error of at most 0.007.
Values may be sent and summed in bfloat16 or wider, within the bound.
No kernel may reach another device: no remote copies, remote signals or barrier semaphores. Data moves between devices by JAX's collectives and lax.ppermute only.
A program may use at most 128 MiB of HBM per device.

v0:
```python
import math
import jax
import jax.numpy as jnp
from jax import lax
from jax.sharding import Mesh
from jax.sharding import PartitionSpec as P

QK = 128
VD = 256
MAXLEN = 8192
lambda_start = 0.8 - 0.6 * math.exp(-3.3)
masked_score = -1e30


def locate(index, lengths):
    ends = jnp.cumsum(lengths)
    starts = ends - lengths
    segment = jnp.sum((ends[None, :] <= index[:, None]).astype(jnp.int32), axis=1)
    hit = jnp.arange(lengths.shape[0], dtype=jnp.int32)[None, :] == segment[:, None]
    begin = jnp.sum(jnp.where(hit, starts[None, :], 0), axis=1)
    return (segment, index - begin)


def rotate(proj, position):
    half = proj.shape[-1] // 2
    freq = 10000.0 ** (-jnp.arange(half, dtype=jnp.float32) / half)
    angle = position.astype(jnp.float32)[:, None] * freq[None, :]
    cosine = jnp.cos(angle)[:, None, None, :]
    sine = jnp.sin(angle)[:, None, None, :]
    front = proj[..., :half]
    back = proj[..., half:]
    return jnp.concatenate([front * cosine - back * sine, back * cosine + front * sine], axis=-1)


def swap_cores(value):
    return lax.ppermute(value, "core", [(0, 1), (1, 0)])


def on_device(tokens, norm_gain, w_query, w_key, w_value, w_out, lambdas, sub_gain, lengths):
    rows = tokens.shape[0]
    heads = w_query.shape[1] // (2 * QK)
    key_cols = heads * 2 * QK
    ys, zs, xs = (lax.axis_size("y"), lax.axis_size("z"), lax.axis_size("x"))
    chips = ys * zs * xs
    total = rows * 2 * chips
    core = lax.axis_index("core")
    chip = (lax.axis_index("y") * zs + lax.axis_index("z")) * xs + lax.axis_index("x")
    first = (chip * 2 + core) * rows
    local_index = first + jnp.arange(rows, dtype=jnp.int32)
    unused, pos_own = locate(local_index, lengths)
    xf = tokens.astype(jnp.float32)
    normed = (xf * lax.rsqrt(jnp.mean(xf * xf, axis=-1, keepdims=True) + 1e-06) * norm_gain).astype(
        jnp.bfloat16
    )
    keys = rotate(
        jnp.dot(normed, w_key, preferred_element_type=jnp.float32).reshape(rows, heads, 2, QK),
        pos_own,
    ).astype(jnp.bfloat16)
    values = jnp.dot(normed, w_value, preferred_element_type=jnp.float32).astype(jnp.bfloat16)
    key_flat = keys.reshape(rows, key_cols)
    lam = (
        jnp.exp(jnp.sum(lambdas[0] * lambdas[1], axis=-1))
        - jnp.exp(jnp.sum(lambdas[2] * lambdas[3], axis=-1))
        + lambda_start
    )
    scale = QK ** (-0.5)

    def head_kv(h):
        k_h = lax.dynamic_index_in_dim(keys, h, axis=1, keepdims=False).reshape(rows, 2 * QK)
        v_h = lax.dynamic_index_in_dim(values.reshape(rows, heads, VD), h, axis=1, keepdims=False)
        return jnp.concatenate([k_h, v_h], axis=1)

    def in_order(mine, theirs, first_is_mine):
        rows_each = mine.shape[0]
        both = jnp.zeros((2 * rows_each,) + mine.shape[1:], mine.dtype)
        both = lax.dynamic_update_slice_in_dim(
            both, mine, jnp.where(first_is_mine, 0, rows_each), axis=0
        )
        return lax.dynamic_update_slice_in_dim(
            both, theirs, jnp.where(first_is_mine, rows_each, 0), axis=0
        )

    span = 2 * rows
    z = lax.axis_index("z")
    kv_both = jnp.stack([head_kv(0), head_kv(1)], axis=1)
    halves = [
        lax.ppermute(kv_both[..., i * 2 * QK : (i + 1) * 2 * QK], "z", [(0, 1), (1, 0)])
        for i in range(2)
    ]
    kv_chips = in_order(kv_both, jnp.concatenate(halves, axis=-1), z == 0)
    mine = lax.dynamic_index_in_dim(kv_chips, core, axis=1, keepdims=False).reshape(2, rows, -1)
    theirs = swap_cores(
        lax.dynamic_index_in_dim(kv_chips, 1 - core, axis=1, keepdims=False)
    ).reshape(2, rows, -1)
    quad = jnp.zeros((2, span, mine.shape[-1]), mine.dtype)
    quad = lax.dynamic_update_slice_in_dim(quad, mine, core * rows, axis=1)
    quad = lax.dynamic_update_slice_in_dim(quad, theirs, (1 - core) * rows, axis=1)
    kv_quad = quad.reshape(2 * span, -1)
    kv_pair = lax.dynamic_index_in_dim(quad, z, axis=0, keepdims=False)
    gathered = lax.all_gather(kv_quad, ("y", "x"), axis=0, tiled=True)
    query = rotate(
        jnp.dot(normed, w_query, preferred_element_type=jnp.float32).reshape(rows, heads, 2, QK),
        pos_own,
    ).astype(jnp.bfloat16)
    q_pair = in_order(
        lax.dynamic_index_in_dim(query, core, axis=1, keepdims=False),
        swap_cores(lax.dynamic_index_in_dim(query, 1 - core, axis=1, keepdims=False)),
        core == 0,
    )
    reach = min(MAXLEN // span, chips - 1)
    window = reach * span
    base = chip * span
    first_chip = jnp.clip(chip - reach, 0, chips - reach)
    start = first_chip * span
    q_index = base + jnp.arange(span, dtype=jnp.int32)
    q_seg, unused = locate(q_index, lengths)

    def stats_of(kv_win, key_index, allowed):
        v_win = kv_win[:, 2 * QK :]
        stats = []
        for m in range(2):
            k_m = kv_win[:, m * QK : (m + 1) * QK]
            scores = (
                jnp.einsum("qd,kd->qk", q_pair[:, m, :], k_m, preferred_element_type=jnp.float32)
                * scale
            )
            scores = jnp.where(allowed, scores, masked_score)
            top = jnp.max(scores, axis=-1, keepdims=True)
            weights = jnp.where(allowed, jnp.exp(scores - top), 0.0)
            mass = jnp.sum(weights, axis=-1, keepdims=True)
            acc = jnp.dot(weights.astype(jnp.bfloat16), v_win, preferred_element_type=jnp.float32)
            stats.append((top, mass, acc))
        return stats

    local_allowed = (q_index[None, :] <= q_index[:, None]) & (q_seg[None, :] == q_seg[:, None])
    local_stats = stats_of(kv_pair, q_index, local_allowed)
    local_stats, gathered = lax.optimization_barrier((local_stats, gathered))
    c = first_chip + jnp.arange(reach, dtype=jnp.int32)
    slot = (c // (zs * xs) * xs + c % xs) * zs + c // xs % zs
    kv_window = jnp.take(gathered.reshape(chips, span, -1), slot, axis=0, mode="clip").reshape(
        window, -1
    )
    pieces = 2
    piece = window // pieces

    def part(p):
        key_index = start + p * piece + jnp.arange(piece, dtype=jnp.int32)
        k_seg, unused = locate(key_index, lengths)
        allowed = (key_index[None, :] < base) & (k_seg[None, :] == q_seg[:, None])
        return stats_of(kv_window[p * piece : (p + 1) * piece], key_index, allowed)

    all_stats = [local_stats] + [part(p) for p in range(pieces)]

    def attend(m):
        tops = [stats[m][0] for stats in all_stats]
        top = tops[0]
        for other in tops[1:]:
            top = jnp.maximum(top, other)
        acc = 0.0
        mass = 0.0
        for stats in all_stats:
            fade = jnp.exp(stats[m][0] - top)
            mass = mass + stats[m][1] * fade
            acc = acc + stats[m][2] * fade
        return acc / mass

    lam_h = lax.dynamic_index_in_dim(lam, core, keepdims=False)
    gain_h = lax.dynamic_index_in_dim(sub_gain, core, axis=0, keepdims=False)
    diff = attend(0) - lam_h * attend(1)
    head_out = (
        diff
        * lax.rsqrt(jnp.mean(diff * diff, axis=-1, keepdims=True) + 1e-05)
        * gain_h
        * (1.0 - lambda_start)
    ).astype(jnp.bfloat16)
    own_rows = lax.dynamic_slice_in_dim(head_out, core * rows, rows, axis=0)
    other_rows = swap_cores(lax.dynamic_slice_in_dim(head_out, (1 - core) * rows, rows, axis=0))
    merged = jnp.where(
        core == 0,
        jnp.concatenate([own_rows, other_rows], axis=1),
        jnp.concatenate([other_rows, own_rows], axis=1),
    )
    summed = lax.psum(
        jnp.dot(merged, w_out, preferred_element_type=jnp.float32).astype(jnp.bfloat16), "tp"
    ).astype(jnp.float32)
    hidden = (xf + summed).astype(jnp.bfloat16)
    return (hidden, key_flat, values)


def solution(mesh):
    req, tp = (mesh.shape["req"], mesh.shape["tp"])
    paired = Mesh(mesh.devices.reshape(req // 16, 2, 4, 2, tp), ("y", "z", "x", "core", "tp"))
    rows = ("y", "z", "x", "core")
    in_specs = (
        P(rows, None),
        P(),
        P(None, "tp"),
        P(None, "tp"),
        P(None, "tp"),
        P("tp", None),
        P(None, "tp", None),
        P("tp", None),
        P(),
    )
    out_specs = (P(rows, None), P(rows, "tp"), P(rows, "tp"))
    return jax.shard_map(
        on_device, mesh=paired, in_specs=in_specs, out_specs=out_specs, check_vma=False
    )
```

profile of v0, /device:TPU:1, one launch (start us, length us, event | category | flops | bytes accessed | tf_op | source)
XLA Modules:
  0.0 296.7 jit_solution(17206890886922927815)
XLA Ops:
  7.3 1.0 reduce-window.8
  8.2 0.7 bitcast_subtract_fusion
  9.1 1.5 fusion.16
  10.6 2.7 fusion.131
  13.3 0.3 reshape.337
  13.7 0.5 multiply_cosine_fusion
  14.2 0.8 multiply_subtract_fusion
  15.0 0.7 maximum_convert_fusion
  15.7 0.8 fusion.136
  16.6 2.7 convolution_convert_fusion.1
  19.3 0.7 copy-done.6
  20.1 0.4 fusion.137
  20.4 0.9 copy.47
  21.5 0.8 fusion.103
  22.2 2.5 collective-permute-start.1
  24.8 5.1 %collective-permute-done.1 = bf16[256,2,256]{2,0,1:T(8,128)(2,1)S(1)} collective-permute-done((bf16[256,2,256]{2,0,1:T(8,128)(2,1)}, bf16[256,2,256]{2,0,1:T(8,128)(2,1)S(1)}, u32[]{:S(2)}, u32[]{:S(2)}) %collective-permute-start.1) | collective-permute-done | bytes 262176 | tf_op jit(solution)/shard_map/ppermute | solution.py:87
  30.0 5.5 %collective-permute-done.2 = bf16[256,2,256]{2,0,1:T(8,128)(2,1)} collective-permute-done((bf16[256,2,256]{2,0,1:T(8,128)(2,1)S(1)}, bf16[256,2,256]{2,0,1:T(8,128)(2,1)}, u32[]{:S(2)}, u32[]{:S(2)}) %collective-permute-start.2) | collective-permute-done | bytes 262176 | tf_op jit(solution)/shard_map/ppermute | solution.py:87
  35.5 1.0 maximum_dynamic-update-slice_fusion
  36.5 1.0 dynamic-slice_bitcast_fusion.1
  37.5 2.4 collective-permute-start.3
  40.0 1.1 constant_dynamic-update-slice_fusion.1
  41.1 0.7 collective-permute-done.3
  41.8 1.1 constant_dynamic-update-slice_fusion
  42.9 1.0 copy-done.1
  43.9 3.6 %fusion.133 = f32[256,512]{1,0:T(8,128)} fusion(bf16[2048,512]{1,0:T(8,128)(2,1)} %param.11, bf16[256,2048]{1,0:T(8,128)(2,1)} %param.9, f32[2048]{0:T(1024)S(1)} %copy-done.16, f32[256]{0:T(256)S(1)} %add_rsqrt_fusion.1), kind=kOutput, calls=%fused_computation.180 | convolution fusion | flops 538968064 | bytes 3679232 | tf_op jit(solution)/shard_map/dot_general | solution.py:102
  47.5 2.2 reshape.336
  49.7 2.0 add_convert_fusion
  51.7 0.7 fusion.113
  52.4 0.7 copy.49
  53.1 0.4 collective-permute-start
  53.5 0.6 broadcast_compare_fusion.1
  54.1 0.6 pad_clamp_fusion
  54.7 0.6 broadcast_compare_fusion
  55.4 0.6 iota_add_fusion
  56.0 1.3 convert_reduce_fusion.2
  57.3 0.5 subtract_add_fusion
  57.9 0.7 copy-done.7
  58.6 0.7 constant_dynamic-slice_fusion.2
  59.3 1.2 dynamic_slice.55
  60.4 0.9 convert_reduce_fusion.1
  61.3 1.6 constant_dynamic-update-slice_fusion.2
  63.0 1.3 fusion.139
  64.3 1.3 fusion.138
  65.6 0.4 fusion.93
  66.1 0.5 fusion.95
  66.6 1.4 fusion.97
  68.0 94.9 %all-gather.2.cloned.1.call-done = bf16[16384,512]{1,0:T(8,128)(2,1)} async-done(((bf16[1024,512]{1,0:T(8,128)(2,1)}), bf16[16384,512]{1,0:T(8,128)(2,1)}) %all-gather.2.cloned.1.call-update) | async-done | bytes 16777232 | tf_op jit(solution)/shard_map/all_gather | solution.py:100
  162.8 10.7 %gather_fusion = bf16[16,512,512]{2,1,0:T(8,128)(2,1)} fusion(bf16[32,512,512]{2,1,0:T(8,128)(2,1)} %bitcast.87, s32[1024]{0:T(1024)} %pad_clamp_fusion), kind=kCustom, calls=%fused_computation | custom fusion | bytes 16777280 | tf_op jit(solution)/shard_map/jit(_take)/gather | solution.py:140
  173.5 3.9 %fusion.135 = (bf16[8,512,512]{2,1,0:T(8,128)(2,1)S(1)}, bf16[8,512,512]{2,1,0:T(8,128)(2,1)S(1)}) fusion(bf16[16,512,512]{2,1,0:T(8,128)(2,1)} %gather_fusion), kind=kLoop, calls=%fused_computation.181 | loop fusion | bytes 16777216 | tf_op jit(solution)/shard_map/slice | solution.py:150
  177.4 2.4 fusion.142
  179.8 2.4 fusion.141
  182.2 4.6 %fusion.143 = (f32[512]{0:T(512)S(1)}, f32[512,4096]{1,0:T(8,128)}) fusion(bf16[4096,512]{1,0:T(8,128)(2,1)S(1)} %bitcast.92, bf16[512,2,128]{2,0,1:T(8,128)(2,1)S(1)} %copy-done.8, s32[512]{0:T(512)S(1)} %copy-done.9, s32[4096]{0:T(1024)S(1)} %get-tuple-element.28, pred[4096]{0:T(1024)(128)(4,1)S(1)} %copy-done.13), kind=kOutput, calls=%fused_computation.189 | convolution fusion | flops 547356160 | bytes 9592832 | tf_op jit(solution)/shard_map/qd,kd->qk/dot_general | solution.py:124
  186.8 3.6 %fusion.140 = (f32[512]{0:T(512)S(1)}, f32[512,4096]{1,0:T(8,128)S(1)}) fusion(bf16[4096,512]{1,0:T(8,128)(2,1)} %bitcast.93, bf16[512,2,128]{2,0,1:T(8,128)(2,1)S(1)} %copy-done.8, s32[512]{0:T(512)S(1)} %copy-done.9, s32[4096]{0:T(1024)S(1)} %get-tuple-element.28, pred[4096]{0:T(1024)(128)(4,1)S(1)} %copy-done.13), kind=kOutput, calls=%fused_computation.186 | convolution fusion | flops 547356160 | bytes 9592832 | tf_op jit(solution)/shard_map/qd,kd->qk/dot_general | solution.py:124
  190.4 11.0 %fusion.4 = (f32[512]{0:T(512)S(1)}, f32[512]{0:T(512)S(1)}, f32[512]{0:T(512)S(1)}, f32[512]{0:T(512)S(1)}) fusion(f32[512,4096]{1,0:T(8,128)S(1)} %get-tuple-element.64, f32[512]{0:T(512)S(1)} %get-tuple-element.63, s32[4096]{0:T(1024)S(1)} %get-tuple-element.27, s32[512]{0:T(512)S(1)} %copy-done.9, pred[4096]{0:T(1024)(128)(4,1)S(1)} %copy-done.12, ...), kind=kLoop, calls=%fused_computation.15 | loop fusion | flops 33552384 | bytes 33613824 | tf_op jit(solution)/shard_map/reduce_sum | solution.py:130
  201.4 5.6 %fusion.61 = f32[512,256]{1,0:T(8,128)S(1)} fusion(bf16[4096,512]{1,0:T(8,128)(2,1)} %bitcast.94, f32[512,4096]{1,0:T(8,128)} %get-tuple-element.68, f32[512]{0:T(512)S(1)} %get-tuple-element.67, s32[4096]{0:T(1024)S(1)} %get-tuple-element.28, s32[512]{0:T(512)S(1)} %copy-done.9, pred[4096]{0:T(1024)(128)(4,1)S(1)} %copy-done.13, f32[512]{0:T(512)S(1)} %bitcast.124), kind=kOutput, calls=%fused_computation.46 | convolution fusion | flops 1084358656 | bytes 11036672 | tf_op jit(solution)/shard_map/dot_general | solution.py:131
  207.1 3.9 %fusion.41 = f32[512,256]{1,0:T(8,128)S(1)} fusion(bf16[4096,512]{1,0:T(8,128)(2,1)} %bitcast.95, f32[512,4096]{1,0:T(8,128)S(1)} %get-tuple-element.62, f32[512]{0:T(512)S(1)} %get-tuple-element.61, s32[4096]{0:T(1024)S(1)} %get-tuple-element.28, s32[512]{0:T(512)S(1)} %copy-done.9, pred[4096]{0:T(1024)(128)(4,1)S(1)} %copy-done.13, f32[512]{0:T(512)S(1)} %bitcast.123), kind=kOutput, calls=%fused_computation.42 | convolution fusion | flops 1084358656 | bytes 11036672 | tf_op jit(solution)/shard_map/dot_general | solution.py:131
  211.1 2.4 fusion.85
  213.4 3.1 %multiply_reduce_fusion = (f32[512]{0:T(512)S(1)}, f32[512,256]{1,0:T(8,128)S(1)}) fusion(f32[512,256]{1,0:T(8,128)S(1)} %fusion.85, f32[512]{0:T(512)S(1)} %bitcast.117, f32[512,256]{1,0:T(8,128)S(1)} %fusion.61, f32[512]{0:T(512)S(1)} %bitcast.119, bf16[4096,512]{1,0:T(8,128)(2,1)S(1)} %bitcast.91, f32[512,4096]{1,0:T(8,128)S(1)} %get-tuple-element.64, ...), kind=kOutput, calls=%fused_computation.74 | convolution fusion | flops 1085406720 | bytes 12615684 | tf_op jit(solution)/shard_map/dot_general | solution.py:131
  216.7 0.8 collective-permute-start.4
  217.5 1.0 collective-permute-done.4
  218.5 1.7 convolution_convert_fusion
  220.2 0.8 convert_element_type.86
  221.0 66.2 %all-reduce.2.cloned.1.call-done = bf16[256,2048]{1,0:T(8,128)(2,1)} async-done(((bf16[256,2048]{1,0:T(8,128)(2,1)}), bf16[256,2048]{1,0:T(8,128)(2,1)}) %all-reduce.2.cloned.1.call-update) | async-done | bytes 1048592 | tf_op jit(solution)/shard_map/psum | solution.py:183
  287.2 2.6 fusion.19
  (64 shorter events, 1.3 us)
Async XLA Ops:
  7.2 211.3 %copy-start = (bf16[512,2048]{1,0:T(8,128)(2,1)S(1)}, bf16[512,2048]{1,0:T(8,128)(2,1)}, u32[]{:S(2)}) copy-start(bf16[512,2048]{1,0:T(8,128)(2,1)} %param.14) | copy-start | bytes 6291460
  7.2 155.7 %all-gather.2.cloned.1.call-start = ((), (), s32[]{:S(2)}) async-start(), calls=%async_computation | async-start | bytes 17825792 | tf_op jit(solution)/shard_map/all_gather | solution.py:100
  8.2 2.4 copy-start.14
  10.6 6.0 %copy-start.16 = (f32[2048]{0:T(1024)S(1)}, f32[2048]{0:T(1024)}, u32[]{:S(2)}) copy-start(f32[2048]{0:T(1024)} %param.10) | copy-start | bytes 24580
  14.2 5.9 %copy-start.5 = (f32[256,64]{1,0:T(8,128)}, f32[256,64]{1,0:T(8,128)S(1)}, u32[]{:S(2)}) copy-start(f32[256,64]{1,0:T(8,128)S(1)} %get-tuple-element.56) | copy-start | bytes 196612
  19.3 0.7 copy-start.6
  22.2 7.8 %collective-permute-start.1 = (bf16[256,2,256]{2,0,1:T(8,128)(2,1)}, bf16[256,2,256]{2,0,1:T(8,128)(2,1)S(1)}, u32[]{:S(2)}, u32[]{:S(2)}) collective-permute-start(bf16[256,2,256]{2,0,1:T(8,128)(2,1)} %get-tuple-element.47), channel_id=1, source_target_pairs={{0,32},{32,0},{1,33},{33,1},{2,34},{34,2},{3,35},{35,3},{4,36},{36... | collective-permute-start | bytes 786440 | tf_op jit(solution)/shard_map/ppermute | solution.py:87
  24.7 10.8 %collective-permute-start.2 = (bf16[256,2,256]{2,0,1:T(8,128)(2,1)S(1)}, bf16[256,2,256]{2,0,1:T(8,128)(2,1)}, u32[]{:S(2)}, u32[]{:S(2)}) collective-permute-start(bf16[256,2,256]{2,0,1:T(8,128)(2,1)S(1)} %get-tuple-element.48), channel_id=1, source_target_pairs={{0,32},{32,0},{1,33},{33,1},{2,34},{34,2},{3,35},{35,3},{4,36},{36... | collective-permute-start | bytes 786440 | tf_op jit(solution)/shard_map/ppermute | solution.py:87
  37.5 4.3 %collective-permute-start.3 = (bf16[512,512]{1,0:T(8,128)(2,1)}, bf16[512,512]{1,0:T(8,128)(2,1)}, u32[]{:S(2)}, u32[]{:S(2)}) collective-permute-start(bf16[512,512]{1,0:T(8,128)(2,1)} %get-tuple-element.39), channel_id=1, source_target_pairs={{0,4},{4,0},{1,5},{5,1},{2,6},{6,2},{3,7},{7,3},{8,12},{12,8},{9,1... | collective-permute-start | bytes 1572872 | tf_op jit(solution)/shard_map/ppermute | solution.py:36
  42.9 1.0 copy-start.1
  43.9 11.4 %copy-start.15 = (f32[4,2,128]{2,1,0:T(2,128)S(1)}, f32[4,2,128]{2,1,0:T(2,128)}, u32[]{:S(2)}) copy-start(f32[4,2,128]{2,1,0:T(2,128)} %param.15) | copy-start | bytes 12292
  43.9 19.1 %copy-start.2 = (bf16[2,512,512]{2,1,0:T(8,128)(2,1)S(1)}, bf16[2,512,512]{2,1,0:T(8,128)(2,1)}, u32[]{:S(2)}) copy-start(bf16[2,512,512]{2,1,0:T(8,128)(2,1)} %copy-done.1) | copy-start | bytes 3145732
  43.9 243.3 %all-reduce.2.cloned.1.call-start = ((), (), s32[]{:S(2)}) async-start(), calls=%async_computation.1 | async-start | bytes 2097152 | tf_op jit(solution)/shard_map/psum | solution.py:183
  53.1 8.3 %collective-permute-start = (bf16[256,2,128]{2,0,1:T(8,128)(2,1)}, bf16[256,2,128]{2,0,1:T(8,128)(2,1)}, u32[]{:S(2)}, u32[]{:S(2)}) collective-permute-start(bf16[256,2,128]{2,0,1:T(8,128)(2,1)} %bitcast.85), channel_id=1, source_target_pairs={{0,4},{4,0},{1,5},{5,1},{2,6},{6,2},{3,7},{7,3},{8,12},{12,8},{9,1... | collective-permute-start | bytes 393224 | tf_op jit(solution)/shard_map/ppermute | solution.py:36
  53.5 4.3 %copy-start.10 = (s32[512]{0:T(512)}, s32[512]{0:T(512)S(1)}, u32[]{:S(2)}) copy-start(s32[512]{0:T(512)S(1)} %iota_add_fusion.2) | copy-start | bytes 6148
  57.9 0.7 copy-start.7
  58.6 7.0 %copy-start.9 = (s32[512]{0:T(512)S(1)}, s32[512]{0:T(512)}, u32[]{:S(2)}) copy-start(s32[512]{0:T(512)} %convert_reduce_fusion.2) | copy-start | bytes 6148
  58.6 7.0 %copy-start.11 = (s32[512]{0:T(512)S(1)}, s32[512]{0:T(512)}, u32[]{:S(2)}) copy-start(s32[512]{0:T(512)} %copy-done.10) | copy-start | bytes 6148
  173.5 3.9 %copy-start.8 = (bf16[512,2,128]{2,0,1:T(8,128)(2,1)S(1)}, bf16[512,2,128]{2,0,1:T(8,128)(2,1)}, u32[]{:S(2)}) copy-start(bf16[512,2,128]{2,0,1:T(8,128)(2,1)} %constant_dynamic-update-slice_fusion.2) | copy-start | bytes 786436
  173.5 3.9 %copy-start.12 = (pred[4096]{0:T(1024)(128)(4,1)S(1)}, pred[4096]{0:T(1024)(128)(4,1)}, u32[]{:S(2)}) copy-start(pred[4096]{0:T(1024)(128)(4,1)} %broadcast_compare_fusion.1) | copy-start | bytes 12292
  177.4 4.8 %copy-start.4 = (bf16[8,512,512]{2,1,0:T(8,128)(2,1)}, bf16[8,512,512]{2,1,0:T(8,128)(2,1)S(1)}, u32[]{:S(2)}) copy-start(bf16[8,512,512]{2,1,0:T(8,128)(2,1)S(1)} %get-tuple-element.38) | copy-start | bytes 12582916
  179.8 2.4 copy-start.13
  207.1 4.0 %copy-start.17 = (f32[512,256]{1,0:T(8,128)S(1)}, f32[512,256]{1,0:T(8,128)}, u32[]{:S(2)}) copy-start(f32[512,256]{1,0:T(8,128)} %fusion.97) | copy-start | bytes 1572868
  216.5 70.7 %copy-start.3 = (bf16[256,2048]{1,0:T(8,128)(2,1)S(1)}, bf16[256,2048]{1,0:T(8,128)(2,1)}, u32[]{:S(2)}) copy-start(bf16[256,2048]{1,0:T(8,128)(2,1)} %param.9) | copy-start | bytes 3145732
  216.7 1.8 collective-permute-start.4
Sparse Core Ops, SparseCore 0:
  44.0 118.7 all-gather.1
  220.3 66.8 all-reduce.1
where the time goes:
time: 297 us
  waiting for transfers between devices  173 us (58%)
  matrix products  43.2 us (15%)
  local copies, waits for them, and re-layouts  30.1 us (10%)
  other arithmetic  29.3 us (10%)
  between operations  14.5 us (5%)
  starting transfers between devices  6.13 us (2%)
    all_gather x1, waiting for transfers between devices, on_device(): gathered = lax.all_gather(kv_quad, ('y', 'x'), axis=0, tiled=True)  94.9 us
    psum x1, waiting for transfers between devices, on_device(): lax.psum(jnp.dot(merged, w_out, preferred_element_type=jnp.float32).astyp...  66.2 us
    dot_general x6, matrix products, stats_of(): jnp.dot(weights.astype(jnp.bfloat16), v_win, preferred_element_type=jnp.f...  17 us
    dot_general x6, matrix products, stats_of(): jnp.einsum('qd,kd->qk', q_pair[:, m, :], k_m, preferred_element_type=jnp....  15.6 us
    reduce_sum x2, other arithmetic, stats_of(): mass = jnp.sum(weights, axis=-1, keepdims=True)  11.4 us
    gather x1, local copies, waits for them, and re-layouts, on_device(): jnp.take(gathered.reshape(chips, span, -1), slot, axis=0, mode='clip')  10.7 us
    ppermute x2, waiting for transfers between devices, on_device(): lax.ppermute(kv_both[..., i * 2 * QK:(i + 1) * 2 * QK], 'z', [(0, 1), (1,...  10.6 us
  transfers between devices with their start and end apart: 7, of which 6 were waited for; matrix products, arithmetic and copies ran while one was open for 8% of the time, Pallas kernels for 0%

commit v1 on v0

--- a/solution.py
+++ b/solution.py
@@ -97,7 +97,9 @@
     quad = lax.dynamic_update_slice_in_dim(quad, theirs, (1 - core) * rows, axis=1)
     kv_quad = quad.reshape(2 * span, -1)
     kv_pair = lax.dynamic_index_in_dim(quad, z, axis=0, keepdims=False)
-    gathered = lax.all_gather(kv_quad, ("y", "x"), axis=0, tiled=True)
+    gathered = jnp.concatenate(
+        lax.all_to_all(jnp.stack([kv_quad] * lax.axis_size(("y", "x"))), ("y", "x"), 0, 0), axis=0
+    )
     query = rotate(
         jnp.dot(normed, w_query, preferred_element_type=jnp.float32).reshape(rows, heads, 2, QK),
         pos_own,

time: 297 us -> 440 us (1.48)
  waiting for transfers between devices: 173 us -> 304 us
  starting transfers between devices: 6.13 us -> 14 us
  local copies, waits for them, and re-layouts: 30.1 us -> 35.1 us
    all_to_all x0 -> x1, waiting for transfers between devices: none -> 227 us  [on_device(): lax.all_to_all(jnp.stack([kv_quad] * lax.axis_size(('y', 'x'))), ('y', 'x...]
    all_gather x1 -> x0, waiting for transfers between devices: 94.9 us -> none  [on_device(): gathered = lax.all_gather(kv_quad, ('y', 'x'), axis=0, tiled=True)]
    all_to_all x0 -> x1, starting transfers between devices: none -> 6.79 us  [on_device(): lax.all_to_all(jnp.stack([kv_quad] * lax.axis_size(('y', 'x'))), ('y', 'x...]
    another operation x0 -> x1, local copies, waits for them, and re-layouts: none -> 5.93 us  [on_device(): jnp.stack([kv_quad] * lax.axis_size(('y', 'x')))]
  transfers between devices with their start and end apart: 7 -> 7, of which waited for: 6 -> 6; matrix products, arithmetic and copies ran while one was open for 8% -> 6% of each run, Pallas kernels for 0% -> 0%
where the time goes in v1:
time: 440 us; the launch traced here: 439 us
  waiting for transfers between devices  304 us (69%)
  matrix products  43.1 us (10%)
  local copies, waits for them, and re-layouts  35.1 us (8%)
  other arithmetic  28.7 us (7%)
  between operations  14.5 us (3%)
  starting transfers between devices  14 us (3%)
    all_to_all x1, waiting for transfers between devices, on_device(): lax.all_to_all(jnp.stack([kv_quad] * lax.axis_size(('y', 'x'))), ('y', 'x...  227 us
    psum x1, waiting for transfers between devices, on_device(): lax.psum(jnp.dot(merged, w_out, preferred_element_type=jnp.float32).astyp...  64.9 us
    dot_general x6, matrix products, stats_of(): jnp.dot(weights.astype(jnp.bfloat16), v_win, preferred_element_type=jnp.f...  17 us
    dot_general x6, matrix products, stats_of(): jnp.einsum('qd,kd->qk', q_pair[:, m, :], k_m, preferred_element_type=jnp....  15.6 us
    reduce_sum x2, other arithmetic, stats_of(): mass = jnp.sum(weights, axis=-1, keepdims=True)  11.4 us
    gather x1, local copies, waits for them, and re-layouts, on_device(): jnp.take(gathered.reshape(chips, span, -1), slot, axis=0, mode='clip')  10.7 us
    ppermute x2, waiting for transfers between devices, on_device(): lax.ppermute(kv_both[..., i * 2 * QK:(i + 1) * 2 * QK], 'z', [(0, 1), (1,...  10.6 us
  transfers between devices with their start and end apart: 7, of which 6 were waited for; matrix products, arithmetic and copies ran while one was open for 6% of the time, Pallas kernels for 0%

profile of v1, /device:TPU:1, one launch (start us, length us, event | category | flops | bytes accessed | tf_op | source)
XLA Modules:
  0.0 439.3 jit_solution(17875728378917444919)
XLA Ops:
  7.2 1.0 reduce-window.8
  8.2 0.7 bitcast_subtract_fusion
  9.0 1.5 fusion.16
  10.6 2.7 fusion.131
  13.3 0.3 reshape.339
  13.6 0.5 multiply_cosine_fusion
  14.2 0.8 multiply_subtract_fusion
  15.0 0.7 maximum_convert_fusion
  15.7 0.8 fusion.136
  16.6 2.7 convolution_convert_fusion.1
  19.2 0.7 copy-done.4
  20.0 0.4 fusion.137
  20.4 0.9 copy.47
  21.4 0.8 fusion.103
  22.2 2.5 collective-permute-start.1
  24.8 5.1 %collective-permute-done.1 = bf16[256,2,256]{2,0,1:T(8,128)(2,1)S(1)} collective-permute-done((bf16[256,2,256]{2,0,1:T(8,128)(2,1)}, bf16[256,2,256]{2,0,1:T(8,128)(2,1)S(1)}, u32[]{:S(2)}, u32[]{:S(2)}) %collective-permute-start.1) | collective-permute-done | bytes 262176 | tf_op jit(solution)/shard_map/ppermute | solution.py:87
  29.9 5.5 %collective-permute-done.2 = bf16[256,2,256]{2,0,1:T(8,128)(2,1)} collective-permute-done((bf16[256,2,256]{2,0,1:T(8,128)(2,1)S(1)}, bf16[256,2,256]{2,0,1:T(8,128)(2,1)}, u32[]{:S(2)}, u32[]{:S(2)}) %collective-permute-start.2) | collective-permute-done | bytes 262176 | tf_op jit(solution)/shard_map/ppermute | solution.py:87
  35.5 1.0 maximum_dynamic-update-slice_fusion
  36.5 1.0 dynamic-slice_bitcast_fusion.1
  37.5 2.4 collective-permute-start.3
  40.0 1.1 constant_dynamic-update-slice_fusion.1
  41.1 0.7 collective-permute-done.3
  41.8 1.1 constant_dynamic-update-slice_fusion
  42.8 5.9 %stack.15 = bf16[16,1024,512]{2,1,0:T(8,128)(2,1)} broadcast(bf16[1024,512]{1,0:T(8,128)(2,1)S(1)} %bitcast.87), dimensions={1,2} | broadcast | bytes 17825792 | tf_op jit(solution)/shard_map/stack | solution.py:101
  48.8 6.8 %all-to-all-start = ((bf16[16,1024,512]{2,1,0:T(8,128)(2,1)}), bf16[16,1024,512]{2,1,0:T(8,128)(2,1)}, u32[]{:S(2)}, u32[]{:S(2)}) async-start(bf16[16,1024,512]{2,1,0:T(8,128)(2,1)} %stack.15), calls=%async_computation | async-start | bytes 33554432 | tf_op jit(solution)/shard_map/all_to_all | solution.py:101
  55.6 3.5 fusion.133
  59.1 2.2 reshape.338
  61.3 2.0 add_convert_fusion
  63.3 0.7 fusion.113
  64.1 0.7 copy.49
  64.7 0.7 collective-permute-start
  65.4 0.6 pad_clamp_fusion
  66.0 0.6 broadcast_compare_fusion
  66.8 0.6 iota_add_fusion
  67.4 1.2 convert_reduce_fusion.2
  68.6 0.5 subtract_add_fusion
  69.2 0.7 copy-done.5
  69.9 0.7 constant_dynamic-slice_fusion.2
  70.6 1.2 dynamic_slice.55
  71.8 0.9 convert_reduce_fusion.1
  72.7 1.6 constant_dynamic-update-slice_fusion.2
  74.3 1.3 fusion.139
  75.6 1.3 fusion.138
  77.0 0.4 fusion.93
  77.4 0.5 fusion.95
  78.0 1.3 fusion.97
  79.3 226.7 %all-to-all-done = bf16[16,1024,512]{2,1,0:T(8,128)(2,1)} async-done(((bf16[16,1024,512]{2,1,0:T(8,128)(2,1)}), bf16[16,1024,512]{2,1,0:T(8,128)(2,1)}, u32[]{:S(2)}, u32[]{:S(2)}) %all-to-all-start) | async-done | bytes 16777248 | tf_op jit(solution)/shard_map/all_to_all | solution.py:101
  306.0 10.7 %gather_fusion = bf16[16,512,512]{2,1,0:T(8,128)(2,1)} fusion(bf16[32,512,512]{2,1,0:T(8,128)(2,1)} %bitcast.20, s32[1024]{0:T(1024)} %pad_clamp_fusion), kind=kCustom, calls=%fused_computation | custom fusion | bytes 16777280 | tf_op jit(solution)/shard_map/jit(_take)/gather | solution.py:142
  316.6 3.9 fusion.135
  320.6 2.4 fusion.142
  322.9 2.4 fusion.141
  325.3 4.6 %fusion.143 = (f32[512]{0:T(512)S(1)}, f32[512,4096]{1,0:T(8,128)}) fusion(bf16[4096,512]{1,0:T(8,128)(2,1)S(1)} %bitcast.92, bf16[512,2,128]{2,0,1:T(8,128)(2,1)S(1)} %copy-done.6, s32[512]{0:T(512)S(1)} %copy-done.7, s32[4096]{0:T(1024)S(1)} %get-tuple-element.28, pred[4096]{0:T(1024)(128)(4,1)S(1)} %copy-done.11), kind=kOutput, calls=%fused_computation.189 | convolution fusion | flops 547356160 | bytes 9592832 | tf_op jit(solution)/shard_map/qd,kd->qk/dot_general | solution.py:126
  329.9 3.6 fusion.140
  333.5 11.0 %fusion.4 = (f32[512]{0:T(512)S(1)}, f32[512]{0:T(512)S(1)}, f32[512]{0:T(512)S(1)}, f32[512]{0:T(512)S(1)}) fusion(f32[512,4096]{1,0:T(8,128)S(1)} %get-tuple-element.64, f32[512]{0:T(512)S(1)} %get-tuple-element.63, s32[4096]{0:T(1024)S(1)} %get-tuple-element.27, s32[512]{0:T(512)S(1)} %copy-done.7, pred[4096]{0:T(1024)(128)(4,1)S(1)} %copy-done.10, ...), kind=kLoop, calls=%fused_computation.15 | loop fusion | flops 33552384 | bytes 33613824 | tf_op jit(solution)/shard_map/reduce_sum | solution.py:132
  344.5 5.6 %fusion.61 = f32[512,256]{1,0:T(8,128)S(1)} fusion(bf16[4096,512]{1,0:T(8,128)(2,1)} %bitcast.94, f32[512,4096]{1,0:T(8,128)} %get-tuple-element.68, f32[512]{0:T(512)S(1)} %get-tuple-element.67, s32[4096]{0:T(1024)S(1)} %get-tuple-element.28, s32[512]{0:T(512)S(1)} %copy-done.7, pred[4096]{0:T(1024)(128)(4,1)S(1)} %copy-done.11, f32[512]{0:T(512)S(1)} %bitcast.124), kind=kOutput, calls=%fused_computation.46 | convolution fusion | flops 1084358656 | bytes 11036672 | tf_op jit(solution)/shard_map/dot_general | solution.py:133
  350.2 3.9 fusion.41
  354.2 2.4 fusion.85
  356.6 3.1 multiply_reduce_fusion
  359.9 1.6 collective-permute-start.4
  361.5 1.0 collective-permute-done.4
  362.5 1.7 convolution_convert_fusion
  364.2 0.8 convert_element_type.86
  365.0 64.9 %all-reduce.2.cloned.1.call-done = bf16[256,2048]{1,0:T(8,128)(2,1)} async-done(((bf16[256,2048]{1,0:T(8,128)(2,1)}), bf16[256,2048]{1,0:T(8,128)(2,1)}) %all-reduce.2.cloned.1.call-update) | async-done | bytes 1048592 | tf_op jit(solution)/shard_map/psum | solution.py:185
  429.9 2.6 fusion.19
  (59 shorter events, 1.2 us)
Async XLA Ops:
  7.2 355.3 %copy-start = (bf16[512,2048]{1,0:T(8,128)(2,1)S(1)}, bf16[512,2048]{1,0:T(8,128)(2,1)}, u32[]{:S(2)}) copy-start(bf16[512,2048]{1,0:T(8,128)(2,1)} %param.14) | copy-start | bytes 6291460
  8.2 2.4 copy-start.12
  10.6 6.0 %copy-start.14 = (f32[2048]{0:T(1024)S(1)}, f32[2048]{0:T(1024)}, u32[]{:S(2)}) copy-start(f32[2048]{0:T(1024)} %param.10) | copy-start | bytes 24580
  14.2 5.9 %copy-start.3 = (f32[256,64]{1,0:T(8,128)}, f32[256,64]{1,0:T(8,128)S(1)}, u32[]{:S(2)}) copy-start(f32[256,64]{1,0:T(8,128)S(1)} %get-tuple-element.56) | copy-start | bytes 196612
  19.2 0.7 copy-start.4
  22.2 7.8 %collective-permute-start.1 = (bf16[256,2,256]{2,0,1:T(8,128)(2,1)}, bf16[256,2,256]{2,0,1:T(8,128)(2,1)S(1)}, u32[]{:S(2)}, u32[]{:S(2)}) collective-permute-start(bf16[256,2,256]{2,0,1:T(8,128)(2,1)} %get-tuple-element.47), channel_id=1, source_target_pairs={{0,32},{32,0},{1,33},{33,1},{2,34},{34,2},{3,35},{35,3},{4,36},{36... | collective-permute-start | bytes 786440 | tf_op jit(solution)/shard_map/ppermute | solution.py:87
  24.7 10.8 %collective-permute-start.2 = (bf16[256,2,256]{2,0,1:T(8,128)(2,1)S(1)}, bf16[256,2,256]{2,0,1:T(8,128)(2,1)}, u32[]{:S(2)}, u32[]{:S(2)}) collective-permute-start(bf16[256,2,256]{2,0,1:T(8,128)(2,1)S(1)} %get-tuple-element.48), channel_id=1, source_target_pairs={{0,32},{32,0},{1,33},{33,1},{2,34},{34,2},{3,35},{35,3},{4,36},{36... | collective-permute-start | bytes 786440 | tf_op jit(solution)/shard_map/ppermute | solution.py:87
  37.5 4.3 collective-permute-start.3
  48.8 257.2 %all-to-all-start = ((bf16[16,1024,512]{2,1,0:T(8,128)(2,1)}), bf16[16,1024,512]{2,1,0:T(8,128)(2,1)}, u32[]{:S(2)}, u32[]{:S(2)}) async-start(bf16[16,1024,512]{2,1,0:T(8,128)(2,1)} %stack.15), calls=%async_computation | async-start | bytes 33554432 | tf_op jit(solution)/shard_map/all_to_all | solution.py:101
  55.6 11.1 %copy-start.13 = (f32[4,2,128]{2,1,0:T(2,128)S(1)}, f32[4,2,128]{2,1,0:T(2,128)}, u32[]{:S(2)}) copy-start(f32[4,2,128]{2,1,0:T(2,128)} %param.15) | copy-start | bytes 12292
  55.6 374.3 %all-reduce.2.cloned.1.call-start = ((), (), s32[]{:S(2)}) async-start(), calls=%async_computation.1 | async-start | bytes 2097152 | tf_op jit(solution)/shard_map/psum | solution.py:185
  64.7 8.0 %collective-permute-start = (bf16[256,2,128]{2,0,1:T(8,128)(2,1)}, bf16[256,2,128]{2,0,1:T(8,128)(2,1)}, u32[]{:S(2)}, u32[]{:S(2)}) collective-permute-start(bf16[256,2,128]{2,0,1:T(8,128)(2,1)} %bitcast.86), channel_id=1, source_target_pairs={{0,4},{4,0},{1,5},{5,1},{2,6},{6,2},{3,7},{7,3},{8,12},{12,8},{9,1... | collective-permute-start | bytes 393224 | tf_op jit(solution)/shard_map/ppermute | solution.py:36
  65.4 3.7 copy-start.8
  69.2 0.7 copy-start.5
  69.9 7.0 %copy-start.7 = (s32[512]{0:T(512)S(1)}, s32[512]{0:T(512)}, u32[]{:S(2)}) copy-start(s32[512]{0:T(512)} %convert_reduce_fusion.2) | copy-start | bytes 6148
  69.9 7.0 %copy-start.9 = (s32[512]{0:T(512)S(1)}, s32[512]{0:T(512)}, u32[]{:S(2)}) copy-start(s32[512]{0:T(512)} %copy-done.8) | copy-start | bytes 6148
  316.6 3.9 copy-start.6
  316.6 3.9 copy-start.10
  320.5 4.8 %copy-start.2 = (bf16[8,512,512]{2,1,0:T(8,128)(2,1)}, bf16[8,512,512]{2,1,0:T(8,128)(2,1)S(1)}, u32[]{:S(2)}) copy-start(bf16[8,512,512]{2,1,0:T(8,128)(2,1)S(1)} %get-tuple-element.38) | copy-start | bytes 12582916
  322.9 2.4 copy-start.11
  350.2 4.0 copy-start.15
  359.7 70.2 %copy-start.1 = (bf16[256,2048]{1,0:T(8,128)(2,1)S(1)}, bf16[256,2048]{1,0:T(8,128)(2,1)}, u32[]{:S(2)}) copy-start(bf16[256,2048]{1,0:T(8,128)(2,1)} %param.9) | copy-start | bytes 3145732
  359.9 2.6 collective-permute-start.4
Sparse Core Ops, SparseCore 0:
  364.3 65.5 all-reduce.1
